TPU v7x, 256 devices: a whole 4x4x8 slice. The times are simulated.
256 devices in a mesh: samp: 32 (over x, z), snp: 8 (over y, core).
Axes of the slice: x: 4, y: 4, z: 8, core: 2. Of those that a mesh axis runs over, the one named last changes fastest.
Arguments:
- dosages: float32 [49152, 8192], P('samp', 'snp'), as said below
- band_counts: int32 [16], P('snp'), may hold values from 1 to 4, as said below
Outputs:
- corr_tiles: float32 [512, 16, 4, 512], P('samp', 'snp')
Inputs may be any that keep to these rules, and one draw needn't show every extreme that they name: b + band_counts[b] <= 16 for every block b, and the counts of all blocks sum to exactly 32. `dosages`: finite real values.
All inputs are finite; a program needn't handle non-finite values.
Results may differ from a plain program's by a relative error of at most 0.0001.
Values sent between devices are 32-bit elements; how exact they have to be, the bound alone decides.
No kernel may reach another device: no remote copies, remote signals or barrier semaphores. Data moves between devices by JAX's collectives and lax.ppermute only.
A program may use at most 192 MiB of HBM per device.

v0:
```python
import jax
import jax.numpy as jnp
from jax import lax
from jax.sharding import PartitionSpec as P

MAXBAND = 4
HIGHEST_MODE = lax.Precision.HIGHEST
epsilon_value = 1e-06
transposed_dims = (((0,), (0,)), ((), ()))


def shifted(value, axis, steps):
    count = lax.axis_size(axis)
    first, last = (max(0, -steps), min(count, count - steps))
    return lax.ppermute(value, axis, [(source, source + steps) for source in range(first, last)])


def on_device(dosages, band_counts):
    samp_rows, column_total = dosages.shape
    blocks_here = band_counts.shape[0]
    block_width = column_total // blocks_here
    band_limit = MAXBAND
    sample_total = samp_rows * lax.axis_size("samp")
    own_rows = block_width // lax.axis_size("samp")
    inverse_total = 1.0 / sample_total
    column_sum = lax.psum(jnp.sum(dosages, axis=0), "samp")
    center = column_sum * inverse_total
    deviation = dosages - center
    square_sum = lax.psum(jnp.sum(deviation * deviation, axis=0), "samp")
    spread = square_sum * inverse_total
    scaled = deviation * lax.rsqrt(spread + epsilon_value)
    band_range = jnp.arange(band_limit, dtype=jnp.int32)
    live_mask = band_range[None, :] < band_counts[:, None]
    reach = (band_limit - 1 + blocks_here - 1) // blocks_here
    sources = [scaled]
    for offset in range(1, reach + 1):
        sources.append(shifted(scaled, "snp", -offset))
    row_list = []
    for local_block in range(blocks_here):
        left_panel = lax.dynamic_slice_in_dim(
            scaled, local_block * block_width, own_rows * lax.axis_size("samp"), 1
        )
        band_list = []
        for band_index in range(band_limit):
            column_block = local_block + band_index
            source = sources[column_block // blocks_here]
            column_start = column_block % blocks_here * block_width
            right_panel = source[:, column_start : column_start + block_width]
            band_list.append(
                lax.dot_general(
                    left_panel,
                    right_panel,
                    transposed_dims,
                    precision=HIGHEST_MODE,
                    preferred_element_type=jnp.float32,
                )
            )
        row_list.append(jnp.stack(band_list, axis=1))
    tile_term = jnp.stack(row_list, axis=1) * inverse_total
    return lax.psum_scatter(
        jnp.where(live_mask[None, :, :, None], tile_term, 0.0),
        "samp",
        scatter_dimension=0,
        tiled=True,
    )


def solution(mesh):
    return jax.shard_map(
        on_device,
        mesh=mesh,
        in_specs=(P("samp", "snp"), P("snp")),
        out_specs=P("samp", "snp", None, None),
        check_vma=False,
    )
```

profile of v0, /device:TPU:8, one launch (start us, length us, event | category | flops | bytes accessed | tf_op | source)
XLA Modules:
  0.0 615.3 jit_solution(15016068143628533306)
XLA Ops:
  6.5 0.0 reduce-scatter.2.cloned.1.call-start
  6.5 3.2 reduce_sum.18
  9.7 77.7 %psum.14 = f32[1024]{0:T(1024)S(1)} all-reduce(f32[1024]{0:T(1024)S(1)} %reduce_sum.18), channel_id=1, replica_groups=mesh['samp'=32,'snp'=8] {'samp'}, use_global_device_ids=true, to_apply=%region_1.0 | all-reduce | flops 1024 | bytes 8192 | tf_op jit(solution)/shard_map/psum | solution.py:26
  87.4 3.5 multiply_reduce_fusion
  90.9 69.6 %psum.15 = f32[1024]{0:T(1024)S(1)} all-reduce(f32[1024]{0:T(1024)S(1)} %multiply_reduce_fusion), channel_id=1, replica_groups=mesh['samp'=32,'snp'=8] {'samp'}, use_global_device_ids=true, to_apply=%region_3.0 | all-reduce | flops 1024 | bytes 8192 | tf_op jit(solution)/shard_map/psum | solution.py:29
  160.5 0.0 copy-start
  160.5 3.6 subtract_multiply_fusion
  164.1 1.9 collective-permute-start
  166.1 2.1 collective-permute-start.1
  168.2 0.0 copy-done
  168.2 0.1 iota_compare_fusion
  168.2 5.3 fusion.26
  173.6 5.3 fusion.23
  178.9 5.5 fusion.29
  184.4 115.6 %collective-permute-done = f32[1536,1024]{1,0:T(8,128)S(1)} collective-permute-done((f32[1536,1024]{1,0:T(8,128)S(1)}, f32[1536,1024]{1,0:T(8,128)S(1)}, u32[]{:S(2)}, u32[]{:S(2)}) %collective-permute-start) | collective-permute-done | bytes 6291488 | tf_op jit(solution)/shard_map/ppermute | solution.py:15
  300.0 5.3 fusion.34
  305.3 5.7 fusion.44
  311.0 0.4 maximum_bitcast_fusion
  311.5 5.3 fusion.39
  316.7 5.5 fusion.49
  322.2 49.2 %collective-permute-done.1 = f32[1536,1024]{1,0:T(8,128)S(1)} collective-permute-done((f32[1536,1024]{1,0:T(8,128)S(1)}, f32[1536,1024]{1,0:T(8,128)S(1)}, u32[]{:S(2)}, u32[]{:S(2)}) %collective-permute-start.1) | collective-permute-done | bytes 6291488 | tf_op jit(solution)/shard_map/ppermute | solution.py:15
  371.4 5.3 fusion.54
  376.7 0.4 maximum_bitcast_fusion.1
  377.1 4.0 fusion
  381.2 0.0 reduce-scatter.2.cloned.1.call-update
  381.2 225.3 %reduce-scatter.2.cloned.1.call-done = f32[16,2,4,512]{3,0,2,1:T(8,128)} async-done(((f32[512,2,4,512]{3,0,2,1:T(8,128)}), f32[16,2,4,512]{3,0,2,1:T(8,128)}) %reduce-scatter.2.cloned.1.call-update) | async-done | bytes 262160 | tf_op jit(solution)/shard_map/reduce_scatter | solution.py:60
  606.5 1.8 copy.3
  (2 shorter events, 0.0 us)
Async XLA Ops:
  6.5 599.9 %reduce-scatter.2.cloned.1.call-start = ((), (), s32[]{:S(2)}) async-start(), calls=%async_computation.1 | async-start | bytes 8650752 | tf_op jit(solution)/shard_map/reduce_scatter | solution.py:60
  160.5 7.6 %copy-start = (s32[2]{0:T(128)S(1)}, s32[2]{0:T(128)}, u32[]{:S(2)}) copy-start(s32[2]{0:T(128)} %param.3) | copy-start | bytes 28
  164.1 135.9 %collective-permute-start = (f32[1536,1024]{1,0:T(8,128)S(1)}, f32[1536,1024]{1,0:T(8,128)S(1)}, u32[]{:S(2)}, u32[]{:S(2)}) collective-permute-start(f32[1536,1024]{1,0:T(8,128)S(1)} %subtract_multiply_fusion), channel_id=1, source_target_pairs={{1,0},{2,1},{3,2},{4,3},{5,4},{6,5},{7,6},{9,8},{10,9},{11,10},{12... | collective-permute-start | bytes 18874376 | tf_op jit(solution)/shard_map/ppermute | solution.py:15
  166.1 205.3 %collective-permute-start.1 = (f32[1536,1024]{1,0:T(8,128)S(1)}, f32[1536,1024]{1,0:T(8,128)S(1)}, u32[]{:S(2)}, u32[]{:S(2)}) collective-permute-start(f32[1536,1024]{1,0:T(8,128)S(1)} %subtract_multiply_fusion), channel_id=1, source_target_pairs={{2,0},{3,1},{4,2},{5,3},{6,4},{7,5},{10,8},{11,9},{12,10},{13,11},... | collective-permute-start | bytes 18874376 | tf_op jit(solution)/shard_map/ppermute | solution.py:15
Sparse Core Ops, SparseCore 0:
  381.3 225.0 reduce-scatter.1
where the time goes:
time: 619 us; the launch traced here: 615 us
  waiting for transfers between devices  390 us (63%)
  blocking collectives  147 us (24%)
  matrix products  43.2 us (7%)
  other arithmetic  15.3 us (2%)
  between operations  13.7 us (2%)
    reduce_scatter x1, waiting for transfers between devices, on_device(): lax.psum_scatter(jnp.where(live_mask[None, :, :, None], tile_term, 0.0),...  225 us
    ppermute x2, waiting for transfers between devices, shifted(): lax.ppermute(value, axis, [(source, source + steps) for source in range(f...  165 us
    psum x1, blocking collectives, on_device(): column_sum = lax.psum(jnp.sum(dosages, axis=0), 'samp')  77.7 us
    psum x1, blocking collectives, on_device(): square_sum = lax.psum(jnp.sum(deviation * deviation, axis=0), 'samp')  69.6 us
    dot_general x8, matrix products, on_device(): lax.dot_general(left_panel, right_panel, transposed_dims, precision=HIGHE...  43.2 us
  transfers between devices with their start and end apart: 3, of which 3 were waited for; matrix products, arithmetic and copies ran while one was open for 6% of the time, Pallas kernels for 0%

commit v1 on v0

--- a/solution.py
+++ b/solution.py
@@ -23,7 +23,7 @@
     sample_total = samp_rows * lax.axis_size("samp")
     own_rows = block_width // lax.axis_size("samp")
     inverse_total = 1.0 / sample_total
-    column_sum = lax.psum(jnp.sum(dosages, axis=0), "samp")
+    column_sum = jnp.sum(lax.all_gather(jnp.sum(dosages, axis=0), "samp"), axis=0)
     center = column_sum * inverse_total
     deviation = dosages - center
     square_sum = lax.psum(jnp.sum(deviation * deviation, axis=0), "samp")

time: 619 us -> 590 us (0.953)
  blocking collectives: 147 us -> 119 us
    psum x1 -> x0, blocking collectives: 77.7 us -> none  [on_device(): column_sum = lax.psum(jnp.sum(dosages, axis=0), 'samp')]
    all_gather x0 -> x1, blocking collectives: none -> 46.4 us  [on_device(): lax.all_gather(jnp.sum(dosages, axis=0), 'samp')]
  transfers between devices with their start and end apart: 3 -> 3, of which waited for: 3 -> 3; matrix products, arithmetic and copies ran while one was open for 6% -> 7% of each run, Pallas kernels for 0% -> 0%
where the time goes in v1:
time: 590 us; the launch traced here: 586 us
  waiting for transfers between devices  389 us (66%)
  blocking collectives  119 us (20%)
  matrix products  43.2 us (7%)
  other arithmetic  15.3 us (3%)
  between operations  13.7 us (2%)
    reduce_scatter x1, waiting for transfers between devices, on_device(): lax.psum_scatter(jnp.where(live_mask[None, :, :, None], tile_term, 0.0),...  224 us
    ppermute x2, waiting for transfers between devices, shifted(): lax.ppermute(value, axis, [(source, source + steps) for source in range(f...  165 us
    psum x1, blocking collectives, on_device(): square_sum = lax.psum(jnp.sum(deviation * deviation, axis=0), 'samp')  72.3 us
    all_gather x1, blocking collectives, on_device(): lax.all_gather(jnp.sum(dosages, axis=0), 'samp')  46.4 us
    dot_general x8, matrix products, on_device(): lax.dot_general(left_panel, right_panel, transposed_dims, precision=HIGHE...  43.2 us
  transfers between devices with their start and end apart: 3, of which 3 were waited for; matrix products, arithmetic and copies ran while one was open for 7% of the time, Pallas kernels for 0%

profile of v1, /device:TPU:8, one launch (start us, length us, event | category | flops | bytes accessed | tf_op | source)
XLA Modules:
  0.0 585.6 jit_solution(4597458159385361926)
XLA Ops:
  6.5 0.0 reduce-scatter.2.cloned.1.call-start
  6.5 3.2 reduce_sum.27
  9.7 46.4 %all-gather = f32[32768]{0:T(1024)S(1)} all-gather(f32[1024]{0:T(1024)S(1)} %reduce_sum.27), channel_id=2, replica_groups=mesh['samp'=32,'snp'=8] {'samp'}, dimensions={0}, use_global_device_ids=true | all-gather | bytes 135168 | tf_op jit(solution)/shard_map/all_gather | solution.py:26
  56.2 3.5 multiply_reduce_fusion
  59.7 72.3 %psum.7 = f32[1024]{0:T(1024)S(1)} all-reduce(f32[1024]{0:T(1024)S(1)} %multiply_reduce_fusion), channel_id=1, replica_groups=mesh['samp'=32,'snp'=8] {'samp'}, use_global_device_ids=true, to_apply=%region_3.0 | all-reduce | flops 1024 | bytes 8192 | tf_op jit(solution)/shard_map/psum | solution.py:29
  132.0 0.0 copy-start
  132.0 3.6 subtract_multiply_fusion
  135.6 1.9 collective-permute-start
  137.5 2.1 collective-permute-start.1
  139.6 0.0 copy-done
  139.6 0.1 iota_compare_fusion
  139.7 5.3 fusion.26
  145.0 5.3 fusion.23
  150.4 5.5 fusion.29
  155.9 115.6 %collective-permute-done = f32[1536,1024]{1,0:T(8,128)S(1)} collective-permute-done((f32[1536,1024]{1,0:T(8,128)S(1)}, f32[1536,1024]{1,0:T(8,128)S(1)}, u32[]{:S(2)}, u32[]{:S(2)}) %collective-permute-start) | collective-permute-done | bytes 6291488 | tf_op jit(solution)/shard_map/ppermute | solution.py:15
  271.5 5.3 fusion.34
  276.8 5.7 fusion.44
  282.5 0.4 maximum_bitcast_fusion
  282.9 5.3 fusion.39
  288.2 5.5 fusion.49
  293.7 49.2 %collective-permute-done.1 = f32[1536,1024]{1,0:T(8,128)S(1)} collective-permute-done((f32[1536,1024]{1,0:T(8,128)S(1)}, f32[1536,1024]{1,0:T(8,128)S(1)}, u32[]{:S(2)}, u32[]{:S(2)}) %collective-permute-start.1) | collective-permute-done | bytes 6291488 | tf_op jit(solution)/shard_map/ppermute | solution.py:15
  342.8 5.3 fusion.54
  348.2 0.4 maximum_bitcast_fusion.1
  348.6 4.0 fusion
  352.6 0.0 reduce-scatter.2.cloned.1.call-update
  352.7 224.1 %reduce-scatter.2.cloned.1.call-done = f32[16,2,4,512]{3,0,2,1:T(8,128)} async-done(((f32[512,2,4,512]{3,0,2,1:T(8,128)}), f32[16,2,4,512]{3,0,2,1:T(8,128)}) %reduce-scatter.2.cloned.1.call-update) | async-done | bytes 262160 | tf_op jit(solution)/shard_map/reduce_scatter | solution.py:60
  576.8 1.8 copy.5
  (4 shorter events, 0.1 us)
Async XLA Ops:
  6.5 570.2 %reduce-scatter.2.cloned.1.call-start = ((), (), s32[]{:S(2)}) async-start(), calls=%async_computation.1 | async-start | bytes 8650752 | tf_op jit(solution)/shard_map/reduce_scatter | solution.py:60
  132.0 7.6 %copy-start = (s32[2]{0:T(128)S(1)}, s32[2]{0:T(128)}, u32[]{:S(2)}) copy-start(s32[2]{0:T(128)} %param.3) | copy-start | bytes 28
  135.6 135.9 %collective-permute-start = (f32[1536,1024]{1,0:T(8,128)S(1)}, f32[1536,1024]{1,0:T(8,128)S(1)}, u32[]{:S(2)}, u32[]{:S(2)}) collective-permute-start(f32[1536,1024]{1,0:T(8,128)S(1)} %subtract_multiply_fusion), channel_id=1, source_target_pairs={{1,0},{2,1},{3,2},{4,3},{5,4},{6,5},{7,6},{9,8},{10,9},{11,10},{12... | collective-permute-start | bytes 18874376 | tf_op jit(solution)/shard_map/ppermute | solution.py:15
  137.5 205.3 %collective-permute-start.1 = (f32[1536,1024]{1,0:T(8,128)S(1)}, f32[1536,1024]{1,0:T(8,128)S(1)}, u32[]{:S(2)}, u32[]{:S(2)}) collective-permute-start(f32[1536,1024]{1,0:T(8,128)S(1)} %subtract_multiply_fusion), channel_id=1, source_target_pairs={{2,0},{3,1},{4,2},{5,3},{6,4},{7,5},{10,8},{11,9},{12,10},{13,11},... | collective-permute-start | bytes 18874376 | tf_op jit(solution)/shard_map/ppermute | solution.py:15
Sparse Core Ops, SparseCore 0:
  352.8 223.9 reduce-scatter.1
